TPU v7x, 32 devices: a whole 2x2x4 slice. The times are simulated.
32 devices in a mesh: groups: 2 (over y), tensor: 4 (over z), seq: 2 (over x), load: 2 (over core).
Axes of the slice: x: 2, y: 2, z: 4, core: 2. Of those that a mesh axis runs over, the one named last changes fastest.
Arguments:
- tokens: bfloat16 [1024, 16384], P(('groups', 'tensor'), ('seq', 'load')), parts along dimension 0, may hold values from -21 to 21
- weight_query: bfloat16 [16384, 16384], P(('seq', 'load'), 'tensor'), may hold values from -0.046875 to 0.046875
- weight_keyval: bfloat16 [16384, 2048], P(('seq', 'load'), 'tensor'), may hold values from -0.046875 to 0.046875
- down_query: bfloat16 [16384, 1024], P(('seq', 'load'), ('groups', 'tensor')), parts along dimension 1, may hold values from -0.046875 to 0.046875
- down_keyval: bfloat16 [16384, 1024], P(('seq', 'load'), ('groups', 'tensor')), parts along dimension 1, may hold values from -0.046875 to 0.046875
- up_query: bfloat16 [1024, 16384], P(('groups', 'load'), 'tensor'), parts along dimension 0, may hold values from -0.5 to 0.5
- up_keyval: bfloat16 [1024, 2048], P(('groups', 'load'), 'tensor'), parts along dimension 0, may hold values from -0.5 to 0.5
- adapter_rank: int32 [8], P('groups'), parts along dimension 0, may hold values from 8 to 128, as said below
- token_lengths: int32 [8], P('groups'), parts along dimension 0, may hold values from 1 to 384, 512 in all
- adapter_slot: int32 [8], P('groups'), parts along dimension 0, may hold values from 0 to 3, each once
Outputs:
- context: bfloat16 [1024, 16384], P(('groups', 'seq', 'load'), 'tensor'), parts along dimension 0
- kv_cache: bfloat16 [1024, 2048], P(('groups', 'seq', 'load'), 'tensor'), parts along dimension 0
There are 2 independent parts, one for each index of `groups`. A program takes and returns all parts, laid end to end along the dimension named above; an argument that names none is the same for every part. Nothing has to cross between parts.
Inputs may be any that keep to these rules, and one draw needn't show every extreme that they name: `adapter_rank`: each rank is a power of two; some tenant has rank 128 and some has rank 8. `token_lengths`: the lengths sum to 512; some tenant has exactly 384 tokens. `adapter_slot`: each slot belongs to exactly one tenant.
All inputs are finite; a program needn't handle non-finite values.
Results may differ from a plain program's by a relative error of at most 0.0025.
The roundings to bfloat16 on the way count: a program that leaves them out, or rounds other values in their place, can miss the bound.
Values may be sent and summed in bfloat16 or wider, within the bound.
No kernel may reach another device: no remote copies, remote signals or barrier semaphores. Data moves between devices by JAX's collectives and lax.ppermute only.
A program may use at most 128 MiB of HBM per device.

v0:
```python
import math
import jax
import jax.numpy as jnp
from jax import lax
from jax.sharding import PartitionSpec as P

HEADS = 128
KV_HEADS = 8
HEAD_DIM = 128
TENANTS = 4
ROPE_BASE = 500000.0
ADAPTER_ALPHA = 8.0


def product(left, right):
    return jnp.dot(left, right, preferred_element_type=jnp.float32)


def rotate_pairs(values, position, first_col):
    pair_count = values.shape[1] // 2
    pair_col = first_col + 2 * jnp.arange(pair_count, dtype=jnp.int32)
    within = pair_col % HEAD_DIM // 2
    frequency = jnp.exp(-(2.0 * within.astype(jnp.float32) / HEAD_DIM) * math.log(ROPE_BASE))
    angles = position.astype(jnp.float32)[:, None] * frequency[None, :]
    pair_view = values.reshape(values.shape[0], pair_count, 2)
    even_part = pair_view[:, :, 0]
    odd_part = pair_view[:, :, 1]
    cosine = jnp.cos(angles)
    sine_angle = jnp.sin(angles)
    turned = jnp.stack(
        [even_part * cosine - odd_part * sine_angle, even_part * sine_angle + odd_part * cosine],
        axis=2,
    )
    return turned.reshape(values.shape)


def tenant_table(token_ids, adapter_rank, token_lengths, adapter_slot):
    segment_ends = jnp.cumsum(token_lengths)
    begins = segment_ends - token_lengths
    owned_rows = (token_ids[:, None] >= begins[None, :]) & (
        token_ids[:, None] < segment_ends[None, :]
    )
    zero_int = jnp.zeros((), jnp.int32)
    own_rank = jnp.sum(jnp.where(owned_rows, adapter_rank[None, :], zero_int), axis=1)
    own_slot = jnp.sum(jnp.where(owned_rows, adapter_slot[None, :], zero_int), axis=1)
    own_first = jnp.sum(jnp.where(owned_rows, begins[None, :], zero_int), axis=1)
    slot_hot = own_slot[:, None] == jnp.arange(TENANTS, dtype=jnp.int32)[None, :]
    return (own_rank, own_first, slot_hot)


def select_slot(down_values, slot_hot):
    shaped = down_values.reshape(down_values.shape[0], -1, TENANTS)
    return jnp.sum(jnp.where(slot_hot[:, None, :], shaped, 0.0), axis=2)


def scale_ranks(picked, own_rank, first_rank):
    rank_index = first_rank + jnp.arange(picked.shape[1], dtype=jnp.int32)
    keep_mask = rank_index[None, :] < own_rank[:, None]
    factor = ADAPTER_ALPHA / jnp.sqrt(own_rank.astype(jnp.float32))
    return jnp.where(keep_mask, picked * factor[:, None], 0.0).astype(jnp.bfloat16)


def widen_slots(low_values, slot_hot):
    wide_rows = jnp.where(
        slot_hot[:, None, :], low_values[:, :, None], jnp.zeros((), low_values.dtype)
    )
    return wide_rows.reshape(low_values.shape[0], -1)


def shards(
    tokens,
    weight_query,
    weight_keyval,
    down_query,
    down_keyval,
    up_query,
    up_keyval,
    adapter_rank,
    token_lengths,
    adapter_slot,
):
    ring = lax.axis_size("tensor")
    split = lax.axis_size(("seq", "load"))
    tensor_index = lax.axis_index("tensor")
    block_index = lax.axis_index(("seq", "load"))
    query_cols = weight_query.shape[1]
    keyval_cols = weight_keyval.shape[1]
    rank_share = down_query.shape[1] // TENANTS
    chunk = tokens.shape[0]
    piece = chunk // split
    local_rows = ring * piece
    up_query_all = lax.all_gather(up_query, "load", axis=0, tiled=True)
    up_keyval_all = lax.all_gather(up_keyval, "load", axis=0, tiled=True)
    shift = [(i, (i + 1) % ring) for i in range(ring)]
    held = tokens
    reduced = []
    for step in range(ring):
        following = lax.ppermute(held, "tensor", shift) if step < ring - 1 else None
        owner = (tensor_index - step) % ring
        block_ids = owner * chunk + jnp.arange(chunk, dtype=jnp.int32)
        _, _, block_hot = tenant_table(block_ids, adapter_rank, token_lengths, adapter_slot)
        partial = jnp.concatenate(
            [
                product(held, weight_query),
                product(held, weight_keyval),
                select_slot(product(held, down_query), block_hot),
                select_slot(product(held, down_keyval), block_hot),
            ],
            axis=1,
        )
        reduced.append(lax.psum_scatter(partial, ("seq", "load"), scatter_dimension=0, tiled=True))
        held = following
    steps_of_owner = (tensor_index - jnp.arange(ring, dtype=jnp.int32)) % ring
    summed = jnp.take(jnp.stack(reduced), steps_of_owner, axis=0).reshape(local_rows, -1)
    owners = jnp.arange(ring, dtype=jnp.int32)
    piece_ids = jnp.arange(piece, dtype=jnp.int32)
    token_ids = (owners[:, None] * chunk + block_index * piece + piece_ids[None, :]).reshape(-1)
    own_rank, own_first, slot_hot = tenant_table(
        token_ids, adapter_rank, token_lengths, adapter_slot
    )
    position = token_ids - own_first
    low_start = query_cols + keyval_cols
    first_rank = tensor_index * rank_share
    low_query = scale_ranks(summed[:, low_start : low_start + rank_share], own_rank, first_rank)
    low_keyval = scale_ranks(summed[:, low_start + rank_share :], own_rank, first_rank)
    low_both = lax.all_gather(jnp.concatenate([low_query, low_keyval], axis=1), "tensor", axis=1)
    full_query = low_both[:, :, :rank_share].reshape(local_rows, -1)
    full_keyval = low_both[:, :, rank_share:].reshape(local_rows, -1)
    wide_query = widen_slots(full_query, slot_hot)
    wide_keyval = widen_slots(full_keyval, slot_hot)
    delta_query = product(wide_query, up_query_all)
    delta_keyval = product(wide_keyval, up_keyval_all)
    query_rows = rotate_pairs(
        summed[:, :query_cols] + delta_query, position, tensor_index * query_cols
    ).astype(jnp.bfloat16)
    keyval = summed[:, query_cols:low_start] + delta_keyval
    kv_first_col = tensor_index * keyval_cols
    is_key = kv_first_col + jnp.arange(keyval_cols, dtype=jnp.int32) < KV_HEADS * HEAD_DIM
    kv_local = jnp.where(
        is_key[None, :], rotate_pairs(keyval, position, kv_first_col), keyval
    ).astype(jnp.bfloat16)
    kv_all = lax.all_gather(kv_local, "tensor", axis=1, tiled=True)
    heads_here = query_cols // HEAD_DIM
    group_size = HEADS // KV_HEADS
    kv_here = max(heads_here // group_size, 1)
    per_kv = heads_here // kv_here
    kv_first = tensor_index * heads_here // group_size
    key_cols = KV_HEADS * HEAD_DIM
    key_heads = lax.dynamic_slice_in_dim(
        kv_all, kv_first * HEAD_DIM, kv_here * HEAD_DIM, 1
    ).reshape(local_rows, kv_here, HEAD_DIM)
    value_heads = lax.dynamic_slice_in_dim(
        kv_all, key_cols + kv_first * HEAD_DIM, kv_here * HEAD_DIM, 1
    ).reshape(local_rows, kv_here, HEAD_DIM)
    both_heads = lax.all_gather(
        jnp.concatenate([key_heads, value_heads], axis=1), ("seq", "load"), axis=0, tiled=True
    )
    piece_keys = both_heads[:, :kv_here]
    piece_values = both_heads[:, kv_here:]
    key_ids = (
        owners[None, :, None] * chunk
        + jnp.arange(split, dtype=jnp.int32)[:, None, None] * piece
        + piece_ids[None, None, :]
    ).reshape(-1)
    grouped = query_rows.reshape(local_rows, kv_here, per_kv, HEAD_DIM)
    visible = (key_ids[None, :] >= own_first[:, None]) & (key_ids[None, :] <= token_ids[:, None])
    scores = jnp.einsum(
        "qghd,kgd->ghqk", grouped, piece_keys, preferred_element_type=jnp.float32
    ) / math.sqrt(HEAD_DIM)
    scores = jnp.where(visible, scores, -1e30)
    row_top = jnp.max(scores, axis=3)
    exp_scores = jnp.where(visible, jnp.exp(scores - row_top[..., None]), 0.0)
    row_total = jnp.sum(exp_scores, axis=3)
    accumulated = jnp.einsum(
        "ghqk,kgd->ghqd",
        exp_scores.astype(jnp.bfloat16),
        piece_values,
        preferred_element_type=jnp.float32,
    )
    context = (accumulated / row_total[..., None]).astype(jnp.bfloat16)
    context = jnp.transpose(context, (2, 0, 1, 3)).reshape(local_rows, query_cols)
    outgoing = jnp.concatenate([context, kv_local], axis=1)
    by_owner = outgoing.reshape(split, ring // split, piece, -1)
    arrived = lax.all_to_all(by_owner, ("seq", "load"), 0, 0)
    placed = jnp.transpose(arrived, (1, 0, 2, 3)).reshape(local_rows, -1)
    return (placed[:, :query_cols], placed[:, query_cols:])


def solution(mesh):
    placed = (
        P(("groups", "tensor"), ("seq", "load")),
        P(("seq", "load"), "tensor"),
        P(("seq", "load"), "tensor"),
        P(("seq", "load"), ("groups", "tensor")),
        P(("seq", "load"), ("groups", "tensor")),
        P(("groups", "load"), "tensor"),
        P(("groups", "load"), "tensor"),
        P("groups"),
        P("groups"),
        P("groups"),
    )
    return jax.shard_map(
        shards,
        mesh=mesh,
        in_specs=placed,
        out_specs=(P(("groups", "seq", "load"), "tensor"), P(("groups", "seq", "load"), "tensor")),
        check_vma=False,
    )
```

profile of v0, /device:TPU:0, one launch (start us, length us, event | category | flops | bytes accessed | tf_op | source)
XLA Modules:
  0.0 315.2 jit_solution(80680660956528715)
XLA Ops:
  9.9 16.9 %fusion.47 = f32[128,4096]{1,0:T(8,128)} fusion(bf16[128,4096]{1,0:T(8,128)(2,1)} %param.10, bf16[4096,4096]{1,0:T(8,128)(2,1)} %param.11), kind=kOutput, calls=%fused_computation.135 | convolution fusion | flops 4294967296 | bytes 36700160 | tf_op jit(solution)/shard_map/dot_general | solution.py:16
  29.1 3.6 %concatenate.26 = f32[128,4672]{1,0:T(8,128)} concatenate(f32[128,4096]{1,0:T(8,128)} %fusion.47, f32[128,512]{1,0:T(8,128)S(1)} %fusion.48, f32[128,32]{1,0:T(8,128)S(1)} %copy.64, f32[128,32]{1,0:T(8,128)S(1)} %copy.65), dimensions={1} | concatenate | bytes 4784128 | tf_op jit(solution)/shard_map/concatenate | solution.py:102
  32.7 3.1 collective-permute-start
  35.8 25.2 %collective-permute-done = bf16[128,4096]{1,0:T(8,128)(2,1)S(1)} collective-permute-done((bf16[128,4096]{1,0:T(8,128)(2,1)S(1)}, bf16[128,4096]{1,0:T(8,128)(2,1)S(1)}, u32[]{:S(2)}, u32[]{:S(2)}) %collective-permute-start) | collective-permute-done | bytes 1048608 | tf_op jit(solution)/shard_map/ppermute | solution.py:98
  63.6 2.9 fusion.52
  66.5 14.3 %fusion.51 = f32[128,4096]{1,0:T(8,128)} fusion(bf16[128,4096]{1,0:T(8,128)(2,1)S(1)} %collective-permute-done, bf16[4096,4096]{1,0:T(8,128)(2,1)} %param.11), kind=kOutput, calls=%fused_computation.139 | convolution fusion | flops 4294967296 | bytes 36700160 | tf_op jit(solution)/shard_map/dot_general | solution.py:16
  80.8 3.6 %concatenate.27 = f32[128,4672]{1,0:T(8,128)} concatenate(f32[128,4096]{1,0:T(8,128)} %fusion.51, f32[128,512]{1,0:T(8,128)S(1)} %fusion.52, f32[128,32]{1,0:T(8,128)S(1)} %copy.66, f32[128,32]{1,0:T(8,128)S(1)} %copy.67), dimensions={1} | concatenate | bytes 4784128 | tf_op jit(solution)/shard_map/concatenate | solution.py:102
  84.7 26.1 %collective-permute-done.1 = bf16[128,4096]{1,0:T(8,128)(2,1)S(1)} collective-permute-done((bf16[128,4096]{1,0:T(8,128)(2,1)S(1)}, bf16[128,4096]{1,0:T(8,128)(2,1)S(1)}, u32[]{:S(2)}, u32[]{:S(2)}) %collective-permute-start.1) | collective-permute-done | bytes 1048608 | tf_op jit(solution)/shard_map/ppermute | solution.py:98
  113.4 3.0 fusion.56
  116.4 14.3 %fusion.55 = f32[128,4096]{1,0:T(8,128)} fusion(bf16[128,4096]{1,0:T(8,128)(2,1)S(1)} %collective-permute-done.1, bf16[4096,4096]{1,0:T(8,128)(2,1)} %param.11), kind=kOutput, calls=%fused_computation.143 | convolution fusion | flops 4294967296 | bytes 36700160 | tf_op jit(solution)/shard_map/dot_general | solution.py:16
  130.7 3.6 %concatenate.28 = f32[128,4672]{1,0:T(8,128)} concatenate(f32[128,4096]{1,0:T(8,128)} %fusion.55, f32[128,512]{1,0:T(8,128)S(1)} %fusion.56, f32[128,32]{1,0:T(8,128)S(1)} %copy.68, f32[128,32]{1,0:T(8,128)S(1)} %copy.69), dimensions={1} | concatenate | bytes 4784128 | tf_op jit(solution)/shard_map/concatenate | solution.py:102
  134.5 25.2 %collective-permute-done.2 = bf16[128,4096]{1,0:T(8,128)(2,1)S(1)} collective-permute-done((bf16[128,4096]{1,0:T(8,128)(2,1)S(1)}, bf16[128,4096]{1,0:T(8,128)(2,1)S(1)}, u32[]{:S(2)}, u32[]{:S(2)}) %collective-permute-start.2) | collective-permute-done | bytes 1048608 | tf_op jit(solution)/shard_map/ppermute | solution.py:98
  162.2 2.9 fusion.60
  165.2 14.3 %fusion.59 = f32[128,4096]{1,0:T(8,128)} fusion(bf16[128,4096]{1,0:T(8,128)(2,1)S(1)} %collective-permute-done.2, bf16[4096,4096]{1,0:T(8,128)(2,1)} %param.11), kind=kOutput, calls=%fused_computation.147 | convolution fusion | flops 4294967296 | bytes 36700160 | tf_op jit(solution)/shard_map/dot_general | solution.py:16
  179.5 3.6 %concatenate.29 = f32[128,4672]{1,0:T(8,128)} concatenate(f32[128,4096]{1,0:T(8,128)} %fusion.59, f32[128,512]{1,0:T(8,128)S(1)} %fusion.60, f32[128,32]{1,0:T(8,128)S(1)} %copy.70, f32[128,32]{1,0:T(8,128)S(1)} %copy.71), dimensions={1} | concatenate | bytes 4784128 | tf_op jit(solution)/shard_map/concatenate | solution.py:102
  188.6 25.8 %reduce-scatter.11.cloned.1.call-done = f32[32,4672]{1,0:T(8,128)} async-done(((f32[128,4672]{1,0:T(8,128)}), f32[32,4672]{1,0:T(8,128)}) %reduce-scatter.11.cloned.1.call-update) | async-done | bytes 598032 | tf_op jit(solution)/shard_map/reduce_scatter | solution.py:111
  220.6 13.5 %all-gather = bf16[128,256]{0,1:T(8,128)(2,1)S(1)} all-gather(bf16[128,64]{0,1:T(8,128)(2,1)S(1)} %copy.72), channel_id=2, replica_groups=mesh['groups'=2,'tensor'=4,'seq'=2,'load'=2] {'tensor'}, dimensions={1}, use_global_device_ids=true | all-gather | bytes 81920 | tf_op jit(solution)/shard_map/all_gather | solution.py:126
  237.2 4.3 %convolution_add_fusion = f32[128,4096]{1,0:T(8,128)} fusion(bf16[128,512]{0,1:T(8,128)(2,1)S(1)} %bitcast.120, bf16[512,4096]{1,0:T(8,128)(2,1)} %all-gather.3.cloned.1.call-done, f32[128,4672]{1,0:T(8,128)S(1)} %bitcast_select_fusion.4), kind=kOutput, calls=%fused_computation.5 | convolution fusion | flops 537395200 | bytes 8519680 | tf_op jit(solution)/shard_map/dot_general | solution.py:16
  249.1 4.2 %fusion.15 = (bf16[128,2048,1]{1,0,2:T(8,128)(2,1)S(1)}, bf16[128,2048,1]{1,0,2:T(8,128)(2,1)S(1)}) fusion(f32[128,2048,1]{1,0,2:T(8,128)S(1)} %copy.97, f32[128,2048,1]{1,0,2:T(8,128)S(1)} %copy.96, f32[2048]{0:T(1024)S(1)} %fusion.35, f32[128]{0:T(128)S(1)} %copy-done.10), kind=kLoop, calls=%fused_computation.24 | loop fusion | flops 2359296 | bytes 3154432 | tf_op jit(solution)/shard_map/convert
  254.4 16.0 %all_gather.21 = bf16[128,2048]{1,0:T(8,128)(2,1)S(1)} all-gather(bf16[128,512]{1,0:T(8,128)(2,1)S(1)} %select_convert_fusion), channel_id=1, replica_groups=mesh['groups'=2,'tensor'=4,'seq'=2,'load'=2] {'tensor'}, dimensions={1}, use_global_device_ids=true | all-gather | bytes 655360 | tf_op jit(solution)/shard_map/all_gather | solution.py:142
  270.9 6.5 %all_gather.22 = bf16[512,4,128]{2,0,1:T(8,128)(2,1)S(1)} all-gather(bf16[128,4,128]{2,0,1:T(8,128)(2,1)S(1)} %pad_maximum_fusion.3), channel_id=1, replica_groups=mesh['groups'=2,'tensor'=4,'seq'=2,'load'=2] {'seq','load'}, dimensions={0}, use_global_device_ids=true | all-gather | bytes 655360 | tf_op jit(solution)/shard_map/all_gather | solution.py:155
  277.4 5.1 %fusion.46 = (f32[2,16,128]{2,1,0:T(8,128)S(1)}, bf16[2,16,128,512]{2,3,1,0:T(8,128)(2,1)}) fusion(pred[128,512]{0,1:T(8,128)(4,1)S(1)} %compare_and_fusion, bf16[128,2,16,128]{0,3,2,1:T(8,128)(2,1)S(1)} %bitcast.114, bf16[512,4,128]{2,0,1:T(8,128)(2,1)S(1)} %all_gather.22), kind=kOutput, calls=%fused_computation.134 | convolution fusion | flops 549454336 | bytes 5652480 | tf_op jit(solution)/shard_map/sub | solution.py:172
  282.5 4.1 %fusion.7 = bf16[128,2,16,128]{3,0,2,1:T(8,128)(2,1)S(1)} fusion(bf16[2,16,128,512]{2,3,1,0:T(8,128)(2,1)} %get-tuple-element.34, f32[128,2,16]{0,2,1:T(8,128)S(1)} %bitcast.138, bf16[512,4,128]{2,0,1:T(8,128)(2,1)S(1)} %all_gather.22), kind=kOutput, calls=%fused_computation.14 | convolution fusion | flops 537919488 | bytes 5521408 | tf_op jit(solution)/shard_map/ghqk,kgd->ghqd/dot_general | solution.py:174
  287.9 18.4 %all_to_all.5 = bf16[4,1,32,4608]{3,2,1,0:T(8,128)(2,1)S(1)} all-to-all(bf16[4,1,32,4608]{3,2,1,0:T(8,128)(2,1)S(1)} %maximum_bitcast_fusion), channel_id=1, replica_groups=mesh['groups'=2,'tensor'=4,'seq'=2,'load'=2] {'seq','load'}, dimensions={0} | all-to-all | bytes 2359296 | tf_op jit(solution)/shard_map/all_to_all | solution.py:184
  (131 shorter events, 38.9 us)
Async XLA Ops:
  8.0 19.5 %copy-start = (bf16[4096,128]{1,0:T(8,128)(2,1)S(1)}, bf16[4096,128]{1,0:T(8,128)(2,1)}, u32[]{:S(2)}) copy-start(bf16[4096,128]{1,0:T(8,128)(2,1)} %param.14) | copy-start | bytes 3145732
  8.0 180.5 %reduce-scatter.5.cloned.1.call-start = ((), (), s32[]{:S(2)}) async-start(), calls=%async_computation.5 | async-start | bytes 3031040 | tf_op jit(solution)/shard_map/reduce_scatter | solution.py:111
  9.9 16.9 %copy-start.2 = (bf16[4096,512]{1,0:T(8,128)(2,1)S(1)}, bf16[4096,512]{1,0:T(8,128)(2,1)}, u32[]{:S(2)}) copy-start(bf16[4096,512]{1,0:T(8,128)(2,1)} %param.12) | copy-start | bytes 12582916
  9.9 16.9 %copy-start.3 = (bf16[128,4096]{1,0:T(8,128)(2,1)S(1)}, bf16[128,4096]{1,0:T(8,128)(2,1)}, u32[]{:S(2)}) copy-start(bf16[128,4096]{1,0:T(8,128)(2,1)} %param.10) | copy-start | bytes 3145732
  26.7 1.4 copy-start.4
  27.5 1.1 copy-start.12
  27.6 1.1 copy-start.13
  32.7 155.9 %reduce-scatter.7.cloned.1.call-start = ((), (), s32[]{:S(2)}) async-start(), calls=%async_computation.6 | async-start | bytes 3031040 | tf_op jit(solution)/shard_map/reduce_scatter | solution.py:111
  32.7 28.3 %collective-permute-start = (bf16[128,4096]{1,0:T(8,128)(2,1)S(1)}, bf16[128,4096]{1,0:T(8,128)(2,1)S(1)}, u32[]{:S(2)}, u32[]{:S(2)}) collective-permute-start(bf16[128,4096]{1,0:T(8,128)(2,1)S(1)} %copy-done.3), channel_id=1, source_target_pairs={{0,4},{4,8},{8,12},{12,0},{1,5},{5,9},{9,13},{13,1},{2,6},{6,10},{... | collective-permute-start | bytes 3145736 | tf_op jit(solution)/shard_map/ppermute | solution.py:98
  84.4 104.1 %reduce-scatter.9.cloned.1.call-start = ((), (), s32[]{:S(2)}) async-start(), calls=%async_computation.7 | async-start | bytes 3031040 | tf_op jit(solution)/shard_map/reduce_scatter | solution.py:111
  84.5 26.4 %collective-permute-start.1 = (bf16[128,4096]{1,0:T(8,128)(2,1)S(1)}, bf16[128,4096]{1,0:T(8,128)(2,1)S(1)}, u32[]{:S(2)}, u32[]{:S(2)}) collective-permute-start(bf16[128,4096]{1,0:T(8,128)(2,1)S(1)} %collective-permute-done), channel_id=1, source_target_pairs={{0,4},{4,8},{8,12},{12,0},{1,5},{5,9},{9,13},{13,1},{2,6},{6,10},{... | collective-permute-start | bytes 3145736 | tf_op jit(solution)/shard_map/ppermute | solution.py:98
  134.3 80.0 %reduce-scatter.11.cloned.1.call-start = ((), (), s32[]{:S(2)}) async-start(), calls=%async_computation.8 | async-start | bytes 3031040 | tf_op jit(solution)/shard_map/reduce_scatter | solution.py:111
  134.4 25.2 %collective-permute-start.2 = (bf16[128,4096]{1,0:T(8,128)(2,1)S(1)}, bf16[128,4096]{1,0:T(8,128)(2,1)S(1)}, u32[]{:S(2)}, u32[]{:S(2)}) collective-permute-start(bf16[128,4096]{1,0:T(8,128)(2,1)S(1)} %collective-permute-done.1), channel_id=1, source_target_pairs={{0,4},{4,8},{8,12},{12,0},{1,5},{5,9},{9,13},{13,1},{2,6},{6,10},{... | collective-permute-start | bytes 3145736 | tf_op jit(solution)/shard_map/ppermute | solution.py:98
  183.1 1.9 copy-start.9
  183.1 54.1 %all-gather.3.cloned.1.call-start = ((), (), s32[]{:S(2)}) async-start(), calls=%async_computation.9 | async-start | bytes 6291456 | tf_op jit(solution)/shard_map/all_gather | solution.py:92
  220.4 14.6 %copy-start.10 = (f32[128]{0:T(128)S(1)}, f32[128]{0:T(128)}, u32[]{:S(2)}) copy-start(f32[128]{0:T(128)} %subtract_convert_fusion) | copy-start | bytes 1540
  234.5 7.0 %copy-start.6 = (f32[128,512]{1,0:T(8,128)}, f32[128,512]{1,0:T(8,128)S(1)}, u32[]{:S(2)}) copy-start(f32[128,512]{1,0:T(8,128)S(1)} %convolution_add_fusion.1) | copy-start | bytes 786436
  246.0 2.4 copy-start.5
  253.4 1.0 copy-start.7
  253.4 1.0 copy-start.8
  253.4 1.0 copy-start.11
  287.8 20.3 %copy-start.1 = (bf16[4096,128]{1,0:T(8,128)(2,1)S(1)}, bf16[4096,128]{1,0:T(8,128)(2,1)}, u32[]{:S(2)}) copy-start(bf16[4096,128]{1,0:T(8,128)(2,1)} %param.14) | copy-start | bytes 3145732
Sparse Core Ops, SparseCore 0:
  32.8 36.1 reduce-scatter.4
  84.6 32.8 reduce-scatter.6
  134.5 31.3 reduce-scatter.8
  183.2 31.1 reduce-scatter.10
Sparse Core Ops, SparseCore 1:
  185.1 11.2 all-gather.2
where the time goes:
time: 316 us; the launch traced here: 315 us
  waiting for transfers between devices  103 us (33%)
  matrix products  91 us (29%)
  blocking collectives  56.9 us (18%)
  local copies, waits for them, and re-layouts  31 us (10%)
  between operations  15.9 us (5%)
  other arithmetic  13.9 us (4%)
  starting transfers between devices  3.57 us (1%)
    dot_general x18, matrix products, product(): return jnp.dot(left, right, preferred_element_type=jnp.float32)  81.8 us
    ppermute x3, waiting for transfers between devices, shards(): following = lax.ppermute(held, 'tensor', shift) if step < ring - 1 else None  76.5 us
    reduce_scatter x4, waiting for transfers between devices, shards(): lax.psum_scatter(partial, ('seq', 'load'), scatter_dimension=0, tiled=True)  25.9 us
    all_to_all x1, blocking collectives, shards(): arrived = lax.all_to_all(by_owner, ('seq', 'load'), 0, 0)  18.4 us
    all_gather x1, blocking collectives, shards(): kv_all = lax.all_gather(kv_local, 'tensor', axis=1, tiled=True)  16 us
    concatenate x4, local copies, waits for them, and re-layouts, shards(): jnp.concatenate([product(held, weight_query), product(held, weight_keyval...  14.3 us
    all_gather x1, blocking collectives, shards(): lax.all_gather(jnp.concatenate([low_query, low_keyval], axis=1), 'tensor'...  13.5 us
    all_gather x1, blocking collectives, shards(): lax.all_gather(jnp.concatenate([key_heads, value_heads], axis=1), ('seq',...  6.51 us
  transfers between devices with their start and end apart: 8, of which 4 were waited for; matrix products, arithmetic and copies ran while one was open for 26% of the time, Pallas kernels for 0%

commit v1 on v0

--- a/solution.py
+++ b/solution.py
@@ -139,7 +139,16 @@
     kv_local = jnp.where(
         is_key[None, :], rotate_pairs(keyval, position, kv_first_col), keyval
     ).astype(jnp.bfloat16)
-    kv_all = lax.all_gather(kv_local, "tensor", axis=1, tiled=True)
+    tile_out, current_value = (jax.lax.axis_size("tensor"), jax.lax.axis_index("tensor"))
+    kv_all, tmp = (kv_local, 1)
+    while tmp < tile_out:
+        left_arr = jax.lax.ppermute(
+            kv_all, "tensor", [(tick, tick ^ tmp) for tick in range(tile_out)]
+        )
+        now = jnp.concatenate([kv_all, left_arr], 1)
+        seen_now = jnp.concatenate([left_arr, kv_all], 1)
+        kv_all = jnp.where(current_value & tmp == 0, now, seen_now)
+        tmp = 2 * tmp
     heads_here = query_cols // HEAD_DIM
     group_size = HEADS // KV_HEADS
     kv_here = max(heads_here // group_size, 1)

time: 316 us -> 307 us (0.972)
  blocking collectives: 56.9 us -> 41 us
  waiting for transfers between devices: 103 us -> 107 us
  starting transfers between devices: 3.57 us -> 7.54 us
    all_gather x1 -> x0, blocking collectives: 16 us -> none  [shards(): kv_all = lax.all_gather(kv_local, 'tensor', axis=1, tiled=True)]
    ppermute x0 -> x2, starting transfers between devices: none -> 3.97 us  [shards(): jax.lax.ppermute(kv_all, 'tensor', [(tick, tick ^ tmp) for tick in range(...]
    ppermute x0 -> x2, waiting for transfers between devices: none -> 3.84 us  [shards(): jax.lax.ppermute(kv_all, 'tensor', [(tick, tick ^ tmp) for tick in range(...]
  transfers between devices with their start and end apart: 8 -> 10, of which waited for: 4 -> 5; matrix products, arithmetic and copies ran while one was open for 26% -> 30% of each run, Pallas kernels for 0% -> 0%
where the time goes in v1:
time: 307 us
  waiting for transfers between devices  107 us (35%)
  matrix products  91 us (30%)
  blocking collectives  41 us (13%)
  local copies, waits for them, and re-layouts  30.3 us (10%)
  between operations  15.9 us (5%)
  other arithmetic  14 us (5%)
  starting transfers between devices  7.54 us (2%)
    dot_general x18, matrix products, product(): return jnp.dot(left, right, preferred_element_type=jnp.float32)  81.8 us
    ppermute x3, waiting for transfers between devices, shards(): following = lax.ppermute(held, 'tensor', shift) if step < ring - 1 else None  76.5 us
    reduce_scatter x4, waiting for transfers between devices, shards(): lax.psum_scatter(partial, ('seq', 'load'), scatter_dimension=0, tiled=True)  25.9 us
    all_to_all x1, blocking collectives, shards(): arrived = lax.all_to_all(by_owner, ('seq', 'load'), 0, 0)  18.4 us
    concatenate x4, local copies, waits for them, and re-layouts, shards(): jnp.concatenate([product(held, weight_query), product(held, weight_keyval...  14.3 us
    all_gather x1, blocking collectives, shards(): lax.all_gather(jnp.concatenate([low_query, low_keyval], axis=1), 'tensor'...  13.5 us
    all_gather x1, blocking collectives, shards(): lax.all_gather(jnp.concatenate([key_heads, value_heads], axis=1), ('seq',...  6.51 us
  transfers between devices with their start and end apart: 10, of which 5 were waited for; matrix products, arithmetic and copies ran while one was open for 30% of the time, Pallas kernels for 0%

profile of v1, /device:TPU:0, one launch (start us, length us, event | category | flops | bytes accessed | tf_op | source)
XLA Modules:
  0.0 306.6 jit_solution(17904640142912354843)
XLA Ops:
  9.9 16.9 %fusion.47 = f32[128,4096]{1,0:T(8,128)} fusion(bf16[128,4096]{1,0:T(8,128)(2,1)} %param.10, bf16[4096,4096]{1,0:T(8,128)(2,1)} %param.11), kind=kOutput, calls=%fused_computation.137 | convolution fusion | flops 4294967296 | bytes 36700160 | tf_op jit(solution)/shard_map/dot_general | solution.py:16
  29.1 3.6 %concatenate.38 = f32[128,4672]{1,0:T(8,128)} concatenate(f32[128,4096]{1,0:T(8,128)} %fusion.47, f32[128,512]{1,0:T(8,128)S(1)} %fusion.48, f32[128,32]{1,0:T(8,128)S(1)} %copy.64, f32[128,32]{1,0:T(8,128)S(1)} %copy.65), dimensions={1} | concatenate | bytes 4784128 | tf_op jit(solution)/shard_map/concatenate | solution.py:102
  32.7 3.1 %collective-permute-start = (bf16[128,4096]{1,0:T(8,128)(2,1)S(1)}, bf16[128,4096]{1,0:T(8,128)(2,1)S(1)}, u32[]{:S(2)}, u32[]{:S(2)}) collective-permute-start(bf16[128,4096]{1,0:T(8,128)(2,1)S(1)} %copy-done.3), channel_id=1, source_target_pairs={{0,4},{4,8},{8,12},{12,0},{1,5},{5,9},{9,13},{13,1},{2,6},{6,10},{... | collective-permute-start | bytes 3145736 | tf_op jit(solution)/shard_map/ppermute | solution.py:98
  35.8 25.2 %collective-permute-done = bf16[128,4096]{1,0:T(8,128)(2,1)S(1)} collective-permute-done((bf16[128,4096]{1,0:T(8,128)(2,1)S(1)}, bf16[128,4096]{1,0:T(8,128)(2,1)S(1)}, u32[]{:S(2)}, u32[]{:S(2)}) %collective-permute-start) | collective-permute-done | bytes 1048608 | tf_op jit(solution)/shard_map/ppermute | solution.py:98
  63.6 2.9 fusion.52
  66.5 14.3 %fusion.51 = f32[128,4096]{1,0:T(8,128)} fusion(bf16[128,4096]{1,0:T(8,128)(2,1)S(1)} %collective-permute-done, bf16[4096,4096]{1,0:T(8,128)(2,1)} %param.11), kind=kOutput, calls=%fused_computation.141 | convolution fusion | flops 4294967296 | bytes 36700160 | tf_op jit(solution)/shard_map/dot_general | solution.py:16
  80.8 3.6 %concatenate.39 = f32[128,4672]{1,0:T(8,128)} concatenate(f32[128,4096]{1,0:T(8,128)} %fusion.51, f32[128,512]{1,0:T(8,128)S(1)} %fusion.52, f32[128,32]{1,0:T(8,128)S(1)} %copy.66, f32[128,32]{1,0:T(8,128)S(1)} %copy.67), dimensions={1} | concatenate | bytes 4784128 | tf_op jit(solution)/shard_map/concatenate | solution.py:102
  84.7 26.1 %collective-permute-done.1 = bf16[128,4096]{1,0:T(8,128)(2,1)S(1)} collective-permute-done((bf16[128,4096]{1,0:T(8,128)(2,1)S(1)}, bf16[128,4096]{1,0:T(8,128)(2,1)S(1)}, u32[]{:S(2)}, u32[]{:S(2)}) %collective-permute-start.1) | collective-permute-done | bytes 1048608 | tf_op jit(solution)/shard_map/ppermute | solution.py:98
  113.4 3.0 fusion.56
  116.4 14.3 %fusion.55 = f32[128,4096]{1,0:T(8,128)} fusion(bf16[128,4096]{1,0:T(8,128)(2,1)S(1)} %collective-permute-done.1, bf16[4096,4096]{1,0:T(8,128)(2,1)} %param.11), kind=kOutput, calls=%fused_computation.145 | convolution fusion | flops 4294967296 | bytes 36700160 | tf_op jit(solution)/shard_map/dot_general | solution.py:16
  130.7 3.6 %concatenate.40 = f32[128,4672]{1,0:T(8,128)} concatenate(f32[128,4096]{1,0:T(8,128)} %fusion.55, f32[128,512]{1,0:T(8,128)S(1)} %fusion.56, f32[128,32]{1,0:T(8,128)S(1)} %copy.68, f32[128,32]{1,0:T(8,128)S(1)} %copy.69), dimensions={1} | concatenate | bytes 4784128 | tf_op jit(solution)/shard_map/concatenate | solution.py:102
  134.5 25.2 %collective-permute-done.2 = bf16[128,4096]{1,0:T(8,128)(2,1)S(1)} collective-permute-done((bf16[128,4096]{1,0:T(8,128)(2,1)S(1)}, bf16[128,4096]{1,0:T(8,128)(2,1)S(1)}, u32[]{:S(2)}, u32[]{:S(2)}) %collective-permute-start.2) | collective-permute-done | bytes 1048608 | tf_op jit(solution)/shard_map/ppermute | solution.py:98
  162.2 2.9 fusion.60
  165.2 14.3 %fusion.59 = f32[128,4096]{1,0:T(8,128)} fusion(bf16[128,4096]{1,0:T(8,128)(2,1)S(1)} %collective-permute-done.2, bf16[4096,4096]{1,0:T(8,128)(2,1)} %param.11), kind=kOutput, calls=%fused_computation.149 | convolution fusion | flops 4294967296 | bytes 36700160 | tf_op jit(solution)/shard_map/dot_general | solution.py:16
  179.5 3.6 %concatenate.41 = f32[128,4672]{1,0:T(8,128)} concatenate(f32[128,4096]{1,0:T(8,128)} %fusion.59, f32[128,512]{1,0:T(8,128)S(1)} %fusion.60, f32[128,32]{1,0:T(8,128)S(1)} %copy.70, f32[128,32]{1,0:T(8,128)S(1)} %copy.71), dimensions={1} | concatenate | bytes 4784128 | tf_op jit(solution)/shard_map/concatenate | solution.py:102
  188.6 25.8 %reduce-scatter.11.cloned.1.call-done = f32[32,4672]{1,0:T(8,128)} async-done(((f32[128,4672]{1,0:T(8,128)}), f32[32,4672]{1,0:T(8,128)}) %reduce-scatter.11.cloned.1.call-update) | async-done | bytes 598032 | tf_op jit(solution)/shard_map/reduce_scatter | solution.py:111
  220.6 13.5 %all-gather = bf16[128,256]{0,1:T(8,128)(2,1)S(1)} all-gather(bf16[128,64]{0,1:T(8,128)(2,1)S(1)} %copy.72), channel_id=2, replica_groups=mesh['groups'=2,'tensor'=4,'seq'=2,'load'=2] {'tensor'}, dimensions={1}, use_global_device_ids=true | all-gather | bytes 81920 | tf_op jit(solution)/shard_map/all_gather | solution.py:126
  236.6 4.3 %convolution_add_fusion = f32[128,4096]{1,0:T(8,128)} fusion(bf16[128,512]{0,1:T(8,128)(2,1)S(1)} %bitcast.120, bf16[512,4096]{1,0:T(8,128)(2,1)} %all-gather.3.cloned.1.call-done, f32[128,4672]{1,0:T(8,128)S(1)} %bitcast_select_fusion.4), kind=kOutput, calls=%fused_computation.5 | convolution fusion | flops 537395200 | bytes 8519680 | tf_op jit(solution)/shard_map/dot_general | solution.py:16
  252.6 4.2 %fusion.15 = (bf16[128,2048,1]{1,0,2:T(8,128)(2,1)S(1)}, bf16[128,2048,1]{1,0,2:T(8,128)(2,1)S(1)}) fusion(f32[128,2048,1]{1,0,2:T(8,128)S(1)} %copy.97, f32[128,2048,1]{1,0,2:T(8,128)S(1)} %copy.96, f32[2048]{0:T(1024)S(1)} %fusion.35, f32[128]{0:T(128)S(1)} %copy-done.7), kind=kLoop, calls=%fused_computation.24 | loop fusion | flops 2359296 | bytes 3154432 | tf_op jit(solution)/shard_map/convert
  257.7 3.8 %collective-permute-done.4 = bf16[128,1024]{1,0:T(8,128)(2,1)S(1)} collective-permute-done((bf16[128,1024]{1,0:T(8,128)(2,1)S(1)}, bf16[128,1024]{1,0:T(8,128)(2,1)S(1)}, u32[]{:S(2)}, u32[]{:S(2)}) %collective-permute-start.4) | collective-permute-done | bytes 262176 | tf_op jit(solution)/shard_map/ppermute | solution.py:145
  262.3 6.5 %all_gather.18 = bf16[512,4,128]{2,0,1:T(8,128)(2,1)S(1)} all-gather(bf16[128,4,128]{2,0,1:T(8,128)(2,1)S(1)} %pad_maximum_fusion.3), channel_id=1, replica_groups=mesh['groups'=2,'tensor'=4,'seq'=2,'load'=2] {'seq','load'}, dimensions={0}, use_global_device_ids=true | all-gather | bytes 655360 | tf_op jit(solution)/shard_map/all_gather | solution.py:164
  268.8 5.1 %fusion.46 = (f32[2,16,128]{2,1,0:T(8,128)S(1)}, bf16[2,16,128,512]{2,3,1,0:T(8,128)(2,1)}) fusion(pred[128,512]{0,1:T(8,128)(4,1)S(1)} %compare_and_fusion, bf16[128,2,16,128]{0,3,2,1:T(8,128)(2,1)S(1)} %bitcast.114, bf16[512,4,128]{2,0,1:T(8,128)(2,1)S(1)} %all_gather.18), kind=kOutput, calls=%fused_computation.136 | convolution fusion | flops 549454336 | bytes 5652480 | tf_op jit(solution)/shard_map/sub | solution.py:181
  273.9 4.1 %fusion.7 = bf16[128,2,16,128]{3,0,2,1:T(8,128)(2,1)S(1)} fusion(bf16[2,16,128,512]{2,3,1,0:T(8,128)(2,1)} %get-tuple-element.34, f32[128,2,16]{0,2,1:T(8,128)S(1)} %bitcast.138, bf16[512,4,128]{2,0,1:T(8,128)(2,1)S(1)} %all_gather.18), kind=kOutput, calls=%fused_computation.14 | convolution fusion | flops 537919488 | bytes 5521408 | tf_op jit(solution)/shard_map/ghqk,kgd->ghqd/dot_general | solution.py:183
  279.2 18.4 %all_to_all.5 = bf16[4,1,32,4608]{3,2,1,0:T(8,128)(2,1)S(1)} all-to-all(bf16[4,1,32,4608]{3,2,1,0:T(8,128)(2,1)S(1)} %maximum_bitcast_fusion), channel_id=1, replica_groups=mesh['groups'=2,'tensor'=4,'seq'=2,'load'=2] {'seq','load'}, dimensions={0} | all-to-all | bytes 2359296 | tf_op jit(solution)/shard_map/all_to_all | solution.py:193
  (130 shorter events, 42.4 us)
Async XLA Ops:
  8.0 19.5 %copy-start = (bf16[4096,128]{1,0:T(8,128)(2,1)S(1)}, bf16[4096,128]{1,0:T(8,128)(2,1)}, u32[]{:S(2)}) copy-start(bf16[4096,128]{1,0:T(8,128)(2,1)} %param.14) | copy-start | bytes 3145732
  8.0 180.5 %reduce-scatter.5.cloned.1.call-start = ((), (), s32[]{:S(2)}) async-start(), calls=%async_computation.5 | async-start | bytes 3031040 | tf_op jit(solution)/shard_map/reduce_scatter | solution.py:111
  9.9 16.9 %copy-start.2 = (bf16[4096,512]{1,0:T(8,128)(2,1)S(1)}, bf16[4096,512]{1,0:T(8,128)(2,1)}, u32[]{:S(2)}) copy-start(bf16[4096,512]{1,0:T(8,128)(2,1)} %param.12) | copy-start | bytes 12582916
  9.9 16.9 %copy-start.3 = (bf16[128,4096]{1,0:T(8,128)(2,1)S(1)}, bf16[128,4096]{1,0:T(8,128)(2,1)}, u32[]{:S(2)}) copy-start(bf16[128,4096]{1,0:T(8,128)(2,1)} %param.10) | copy-start | bytes 3145732
  26.7 1.4 copy-start.4
  27.5 1.1 copy-start.9
  27.6 1.1 copy-start.10
  32.7 155.9 %reduce-scatter.7.cloned.1.call-start = ((), (), s32[]{:S(2)}) async-start(), calls=%async_computation.6 | async-start | bytes 3031040 | tf_op jit(solution)/shard_map/reduce_scatter | solution.py:111
  32.7 28.3 %collective-permute-start = (bf16[128,4096]{1,0:T(8,128)(2,1)S(1)}, bf16[128,4096]{1,0:T(8,128)(2,1)S(1)}, u32[]{:S(2)}, u32[]{:S(2)}) collective-permute-start(bf16[128,4096]{1,0:T(8,128)(2,1)S(1)} %copy-done.3), channel_id=1, source_target_pairs={{0,4},{4,8},{8,12},{12,0},{1,5},{5,9},{9,13},{13,1},{2,6},{6,10},{... | collective-permute-start | bytes 3145736 | tf_op jit(solution)/shard_map/ppermute | solution.py:98
  84.4 104.1 %reduce-scatter.9.cloned.1.call-start = ((), (), s32[]{:S(2)}) async-start(), calls=%async_computation.7 | async-start | bytes 3031040 | tf_op jit(solution)/shard_map/reduce_scatter | solution.py:111
  84.5 26.4 %collective-permute-start.1 = (bf16[128,4096]{1,0:T(8,128)(2,1)S(1)}, bf16[128,4096]{1,0:T(8,128)(2,1)S(1)}, u32[]{:S(2)}, u32[]{:S(2)}) collective-permute-start(bf16[128,4096]{1,0:T(8,128)(2,1)S(1)} %collective-permute-done), channel_id=1, source_target_pairs={{0,4},{4,8},{8,12},{12,0},{1,5},{5,9},{9,13},{13,1},{2,6},{6,10},{... | collective-permute-start | bytes 3145736 | tf_op jit(solution)/shard_map/ppermute | solution.py:98
  134.3 80.0 %reduce-scatter.11.cloned.1.call-start = ((), (), s32[]{:S(2)}) async-start(), calls=%async_computation.8 | async-start | bytes 3031040 | tf_op jit(solution)/shard_map/reduce_scatter | solution.py:111
  134.4 25.2 %collective-permute-start.2 = (bf16[128,4096]{1,0:T(8,128)(2,1)S(1)}, bf16[128,4096]{1,0:T(8,128)(2,1)S(1)}, u32[]{:S(2)}, u32[]{:S(2)}) collective-permute-start(bf16[128,4096]{1,0:T(8,128)(2,1)S(1)} %collective-permute-done.1), channel_id=1, source_target_pairs={{0,4},{4,8},{8,12},{12,0},{1,5},{5,9},{9,13},{13,1},{2,6},{6,10},{... | collective-permute-start | bytes 3145736 | tf_op jit(solution)/shard_map/ppermute | solution.py:98
  183.1 1.9 copy-start.6
  183.1 53.5 %all-gather.3.cloned.1.call-start = ((), (), s32[]{:S(2)}) async-start(), calls=%async_computation.9 | async-start | bytes 6291456 | tf_op jit(solution)/shard_map/all_gather | solution.py:92
  220.4 14.6 %copy-start.7 = (f32[128]{0:T(128)S(1)}, f32[128]{0:T(128)}, u32[]{:S(2)}) copy-start(f32[128]{0:T(128)} %subtract_convert_fusion) | copy-start | bytes 1540
  240.9 1.9 copy-start.8
  242.8 7.2 %collective-permute-start.3 = (bf16[128,512]{1,0:T(8,128)(2,1)S(1)}, bf16[128,512]{1,0:T(8,128)(2,1)S(1)}, u32[]{:S(2)}, u32[]{:S(2)}) collective-permute-start(bf16[128,512]{1,0:T(8,128)(2,1)S(1)} %select_convert_fusion), channel_id=1, source_target_pairs={{0,4},{4,0},{8,12},{12,8},{1,5},{5,1},{9,13},{13,9},{2,6},{6,2},{1... | collective-permute-start | bytes 393224 | tf_op jit(solution)/shard_map/ppermute | solution.py:145
  246.9 2.4 copy-start.5
  250.2 11.4 %collective-permute-start.4 = (bf16[128,1024]{1,0:T(8,128)(2,1)S(1)}, bf16[128,1024]{1,0:T(8,128)(2,1)S(1)}, u32[]{:S(2)}, u32[]{:S(2)}) collective-permute-start(bf16[128,1024]{1,0:T(8,128)(2,1)S(1)} %maximum_select_fusion.1), channel_id=1, source_target_pairs={{0,8},{4,12},{8,0},{12,4},{1,9},{5,13},{9,1},{13,5},{2,10},{6,14},... | collective-permute-start | bytes 786440 | tf_op jit(solution)/shard_map/ppermute | solution.py:145
  279.1 20.3 %copy-start.1 = (bf16[4096,128]{1,0:T(8,128)(2,1)S(1)}, bf16[4096,128]{1,0:T(8,128)(2,1)}, u32[]{:S(2)}) copy-start(bf16[4096,128]{1,0:T(8,128)(2,1)} %param.14) | copy-start | bytes 3145732
Sparse Core Ops, SparseCore 0:
  32.8 36.1 reduce-scatter.4
  84.6 32.8 reduce-scatter.6
  134.5 31.3 reduce-scatter.8
  183.2 31.1 reduce-scatter.10
Sparse Core Ops, SparseCore 1:
  185.1 11.2 all-gather.2
